TPU v7x, 256 devices: a whole 4x4x8 slice. The times are simulated.
256 devices in a mesh: sub: 64 (over z, x, core), row: 4 (over y).
Axes of the slice: x: 4, y: 4, z: 8, core: 2. Of those that a mesh axis runs over, the one named last changes fastest.
Arguments:
- residual: float32 [32, 64, 2048], P(None, 'sub', 'row')
- factor: float32 [64, 3072, 3072], P('sub', 'row'), may hold values from -0.0390625 to 0.0390625
- basis: float32 [96, 64, 2048], P(None, 'sub', 'row'), may hold values from -0.015625 to 0.015625
- send_rows: int32 [64, 2, 512], P('sub'), may hold values from 0 to 2047, as said below
Outputs:
- coeffs: float32 [96, 32], replicated
- rfactor: float32 [32, 32], replicated
- block_q: float32 [32, 64, 2048], P(None, 'sub', 'row')
Inputs may be any that keep to these rules, and one draw needn't show every extreme that they name: Within each send_rows[s, side, :] the rows are distinct.
All inputs are finite; a program needn't handle non-finite values.
Results may differ from a plain program's by a relative error of at most 0.000073.
Values sent between devices are 32-bit elements; how exact they have to be, the bound alone decides.
No kernel may reach another device: no remote copies, remote signals or barrier semaphores. Data moves between devices by JAX's collectives and lax.ppermute only.
A program may use at most 64 MiB of HBM per device.

v0:
```python
import jax
import jax.numpy as jnp
from jax import lax
from jax.sharding import PartitionSpec as P

HIGH = lax.Precision.HIGHEST


def from_behind(value, axis, steps):
    count = lax.axis_size(axis)
    leading, last = (max(0, -steps), min(count, count - steps))
    return lax.ppermute(value, axis, [(source, source + steps) for source in range(leading, last)])


def contract_rows(left_mat, right_mat):
    return lax.dot_general(left_mat, right_mat, (((1,), (1,)), ((), ())), precision=HIGH)


def contract_first(left_mat, right_mat):
    return lax.dot_general(left_mat, right_mat, (((0,), (0,)), ((), ())), precision=HIGH)


def second_sum(inner):
    return lax.psum(inner, ("sub", "row"))


def per_device(residual, factor, basis, send_rows):
    slab = residual.shape[2]
    row_count = lax.axis_size("row")
    sub_rows = slab * row_count
    total_rows = sub_rows * lax.axis_size("sub")
    own_rows = residual[:, 0, :]
    whole = lax.all_gather(own_rows, "row", axis=1, tiled=True)
    index_rows = send_rows[0]
    to_lower = jnp.take(whole, index_rows[0], axis=1)
    to_upper = jnp.take(whole, index_rows[1], axis=1)
    from_lower = from_behind(to_upper, "sub", 1)
    from_upper = from_behind(to_lower, "sub", -1)
    extended = jnp.concatenate([whole, from_lower, from_upper], axis=1)
    factor_rows = factor[0]
    share = factor_rows.shape[0]
    margin = from_lower.shape[1]
    row_pos = lax.axis_index("row")
    global_rows = row_pos * share + lax.iota(jnp.int32, share)
    columns = lax.iota(jnp.int32, factor_rows.shape[1])
    full = factor_rows + (global_rows[:, None] == columns[None, :]).astype(jnp.float32)
    inner = contract_rows(extended, full)
    partial_value = jnp.dot(inner, full, precision=HIGH)
    summed = lax.psum(partial_value, "row")
    mine = lax.dynamic_slice_in_dim(summed, row_pos * slab, slab, 1)
    margins = summed[:, sub_rows:]
    back_upper = from_behind(margins[:, :margin], "sub", -1)
    back_lower = from_behind(margins[:, margin:], "sub", 1)
    my_rows = row_pos * slab + lax.iota(jnp.int32, slab)
    select_upper = (index_rows[1][:, None] == my_rows[None, :]).astype(jnp.float32)
    select_lower = (index_rows[0][:, None] == my_rows[None, :]).astype(jnp.float32)
    block_t = (
        mine
        + jnp.dot(back_upper, select_upper, precision=HIGH)
        + jnp.dot(back_lower, select_lower, precision=HIGH)
    )
    vectors = basis[:, 0, :]
    first = lax.psum(contract_rows(vectors, block_t), ("sub", "row"))
    once = block_t - contract_first(first, vectors)
    inner_two = contract_rows(vectors, once)
    second = second_sum(inner_two)
    twice = once - contract_first(second, vectors)
    gram = lax.psum(contract_rows(twice, twice), ("sub", "row")) / total_rows
    lower_tri = jnp.linalg.cholesky(gram)
    solved = jax.scipy.linalg.solve_triangular(lower_tri, twice, lower=True)
    return (first + second, lower_tri.T, solved[:, None, :])


def solution(mesh):
    placed = (
        P(None, "sub", "row"),
        P("sub", "row", None),
        P(None, "sub", "row"),
        P("sub", None, None),
    )
    return jax.shard_map(
        per_device,
        mesh=mesh,
        in_specs=placed,
        out_specs=(P(), P(), P(None, "sub", "row")),
        check_vma=False,
    )
```

profile of v0, /device:TPU:1, one launch (start us, length us, event | category | flops | bytes accessed | tf_op | source)
XLA Modules:
  0.0 366.8 jit_solution(2224883184185922251)
XLA Ops:
  7.2 0.0 all-reduce.2.cloned.1.call-start
  7.2 0.8 fusion.30
  8.0 1.0 copy.12
  9.0 14.5 %all-gather = f32[32,1,2048]{0,2,1:T(8,128)S(1)} all-gather(f32[32,1,512]{0,2,1:T(8,128)S(1)} %copy.12), channel_id=2, replica_groups=mesh['sub'=64,'row'=4] {'row'}, dimensions={2}, use_global_device_ids=true | all-gather | bytes 327680 | tf_op jit(solution)/shard_map/all_gather | solution.py:33
  23.5 1.0 gather_fusion
  24.5 0.1 select_bitcast_fusion.1
  24.6 5.2 %collective-permute-start = (f32[32,512]{0,1:T(8,128)S(1)}, f32[32,512]{0,1:T(8,128)S(1)}, u32[]{:S(2)}, u32[]{:S(2)}) collective-permute-start(f32[32,512]{0,1:T(8,128)S(1)} %select_bitcast_fusion.1), channel_id=1, source_target_pairs={{0,4},{4,8},{8,12},{12,16},{16,20},{20,24},{24,28},{28,32},{32,36}... | collective-permute-start | bytes 196616 | tf_op jit(solution)/shard_map/ppermute | solution.py:12
  29.8 1.0 gather_fusion.1
  30.9 0.1 select_bitcast_fusion
  31.0 1.9 collective-permute-start.1
  33.0 0.3 copy.13
  33.3 0.0 collective-permute-done
  33.3 0.1 copy.14
  33.4 5.3 %collective-permute-done.1 = f32[32,512]{0,1:T(8,128)S(1)} collective-permute-done((f32[32,512]{0,1:T(8,128)S(1)}, f32[32,512]{0,1:T(8,128)S(1)}, u32[]{:S(2)}, u32[]{:S(2)}) %collective-permute-start.1) | collective-permute-done | bytes 65568 | tf_op jit(solution)/shard_map/ppermute | solution.py:12
  38.7 0.1 copy.15
  38.8 0.0 copy-start
  38.8 0.0 copy-start.1
  38.8 11.7 %fusion.1 = f32[32,768]{1,0:T(8,128)S(1)} fusion(f32[1,768,3072]{2,1,0:T(8,128)} %param.7, s32[768]{0:T(1024)S(1)} %iota_add_fusion, f32[32,512]{1,0:T(8,128)S(1)} %copy.15, f32[32,512]{1,0:T(8,128)S(1)} %copy.14, f32[32,2048]{1,0:T(8,128)S(1)} %copy.13), kind=kOutput, calls=%fused_computation.5 | convolution fusion | flops 913244160 | bytes 9931776 | tf_op jit(solution)/shard_map/dot_general | solution.py:16
  50.6 0.0 copy-done
  50.6 7.4 %fusion = f32[32,3072]{1,0:T(8,128)} fusion(f32[32,768]{1,0:T(8,128)S(1)} %fusion.1, f32[1,768,3072]{2,1,0:T(8,128)S(1)} %copy-done, s32[768]{0:T(1024)S(1)} %iota_add_fusion), kind=kOutput, calls=%fused_computation.4 | convolution fusion | flops 913047552 | bytes 9931776 | tf_op jit(solution)/shard_map/dot_general | solution.py:48
  58.0 0.0 all-reduce.2.cloned.1.call-update
  58.0 50.1 %all-reduce.2.cloned.1.call-done = f32[32,3072]{1,0:T(8,128)} async-done(((f32[32,3072]{1,0:T(8,128)}), f32[32,3072]{1,0:T(8,128)}) %all-reduce.2.cloned.1.call-update) | async-done | bytes 393232 | tf_op jit(solution)/shard_map/psum | solution.py:49
  108.2 0.9 fusion.29
  109.1 5.8 %collective-permute-start.3 = (f32[32,512]{1,0:T(8,128)S(1)}, f32[32,512]{1,0:T(8,128)S(1)}, u32[]{:S(2)}, u32[]{:S(2)}) collective-permute-start(f32[32,512]{1,0:T(8,128)S(1)} %get-tuple-element.11), channel_id=1, source_target_pairs={{0,4},{4,8},{8,12},{12,16},{16,20},{20,24},{24,28},{28,32},{32,36}... | collective-permute-start | bytes 196616 | tf_op jit(solution)/shard_map/ppermute | solution.py:12
  114.9 2.1 collective-permute-start.2
  117.0 0.0 collective-permute-done.3
  117.0 0.5 fusion.5
  117.5 3.0 collective-permute-done.2
  120.5 1.4 fusion.4
  121.9 0.0 copy-done.1
  121.9 0.3 convolution_bitcast_fusion.2
  122.2 80.5 %psum.29 = f32[96,32]{0,1:T(8,128)S(1)} all-reduce(f32[96,32]{0,1:T(8,128)S(1)} %convolution_bitcast_fusion.2), channel_id=1, replica_groups=mesh['sub'=64,'row'=4] {'sub','row'}, use_global_device_ids=true, to_apply=%region_1.3 | all-reduce | flops 3072 | bytes 24576 | tf_op jit(solution)/shard_map/psum | solution.py:63
  202.7 0.2 convolution_subtract_fusion.1
  202.9 0.3 convolution_bitcast_fusion.1
  203.3 72.9 %psum.30 = f32[96,32]{0,1:T(8,128)S(1)} all-reduce(f32[96,32]{0,1:T(8,128)S(1)} %convolution_bitcast_fusion.1), channel_id=1, replica_groups=mesh['sub'=64,'row'=4] {'sub','row'}, use_global_device_ids=true, to_apply=%region_2.4 | all-reduce | flops 3072 | bytes 24576 | tf_op jit(solution)/shard_map/psum | solution.py:24
  276.1 0.2 convolution_subtract_fusion
  276.4 0.6 add.69
  277.0 0.2 fusion.31
  277.2 74.4 %psum.31 = f32[32,32]{0,1:T(8,128)S(1)} all-reduce(f32[32,32]{0,1:T(8,128)S(1)} %fusion.31), channel_id=1, replica_groups=mesh['sub'=64,'row'=4] {'sub','row'}, use_global_device_ids=true, to_apply=%region_3.5 | all-reduce | flops 1024 | bytes 8192 | tf_op jit(solution)/shard_map/psum | solution.py:68
  351.5 0.1 copy.17
  351.6 2.9 cholesky.18
  354.6 0.6 compare_reduce_fusion
  355.2 0.7 select_bitcast_fusion.2
  355.9 2.4 custom-call.7
  358.3 0.3 convolution_bitcast_fusion
  358.6 0.7 copy.19
  359.3 0.7 copy.18
  (11 shorter events, 0.1 us)
Async XLA Ops:
  7.2 101.0 %all-reduce.2.cloned.1.call-start = ((), (), s32[]{:S(2)}) async-start(), calls=%async_computation | async-start | bytes 786432 | tf_op jit(solution)/shard_map/psum | solution.py:49
  24.6 8.6 %collective-permute-start = (f32[32,512]{0,1:T(8,128)S(1)}, f32[32,512]{0,1:T(8,128)S(1)}, u32[]{:S(2)}, u32[]{:S(2)}) collective-permute-start(f32[32,512]{0,1:T(8,128)S(1)} %select_bitcast_fusion.1), channel_id=1, source_target_pairs={{0,4},{4,8},{8,12},{12,16},{16,20},{20,24},{24,28},{28,32},{32,36}... | collective-permute-start | bytes 196616 | tf_op jit(solution)/shard_map/ppermute | solution.py:12
  31.0 7.7 %collective-permute-start.1 = (f32[32,512]{0,1:T(8,128)S(1)}, f32[32,512]{0,1:T(8,128)S(1)}, u32[]{:S(2)}, u32[]{:S(2)}) collective-permute-start(f32[32,512]{0,1:T(8,128)S(1)} %select_bitcast_fusion), channel_id=1, source_target_pairs={{4,0},{8,4},{12,8},{16,12},{20,16},{24,20},{28,24},{32,28},{36,32}... | collective-permute-start | bytes 196616 | tf_op jit(solution)/shard_map/ppermute | solution.py:12
  38.8 11.8 %copy-start = (f32[1,768,3072]{2,1,0:T(8,128)S(1)}, f32[1,768,3072]{2,1,0:T(8,128)}, u32[]{:S(2)}) copy-start(f32[1,768,3072]{2,1,0:T(8,128)} %param.7) | copy-start | bytes 28311556
  38.8 83.0 %copy-start.1 = (f32[96,1,512]{2,1,0:T(1,128)S(1)}, f32[96,1,512]{2,1,0:T(1,128)}, u32[]{:S(2)}) copy-start(f32[96,1,512]{2,1,0:T(1,128)} %param.8) | copy-start | bytes 589828
  109.1 8.0 %collective-permute-start.3 = (f32[32,512]{1,0:T(8,128)S(1)}, f32[32,512]{1,0:T(8,128)S(1)}, u32[]{:S(2)}, u32[]{:S(2)}) collective-permute-start(f32[32,512]{1,0:T(8,128)S(1)} %get-tuple-element.11), channel_id=1, source_target_pairs={{0,4},{4,8},{8,12},{12,16},{16,20},{20,24},{24,28},{28,32},{32,36}... | collective-permute-start | bytes 196616 | tf_op jit(solution)/shard_map/ppermute | solution.py:12
  114.9 5.6 %collective-permute-start.2 = (f32[32,512]{1,0:T(8,128)S(1)}, f32[32,512]{1,0:T(8,128)S(1)}, u32[]{:S(2)}, u32[]{:S(2)}) collective-permute-start(f32[32,512]{1,0:T(8,128)S(1)} %get-tuple-element.10), channel_id=1, source_target_pairs={{4,0},{8,4},{12,8},{16,12},{20,16},{24,20},{28,24},{32,28},{36,32}... | collective-permute-start | bytes 196616 | tf_op jit(solution)/shard_map/ppermute | solution.py:12
Sparse Core Ops, SparseCore 0:
  58.2 49.9 all-reduce.1
where the time goes:
time: 368 us; the launch traced here: 367 us
  blocking collectives  242 us (66%)
  waiting for transfers between devices  58.4 us (16%)
  matrix products  22.6 us (6%)
  starting transfers between devices  15 us (4%)
  between operations  14.3 us (4%)
  other arithmetic  7.62 us (2%)
  local copies, waits for them, and re-layouts  6.65 us (2%)
    psum x1, blocking collectives, per_device(): first = lax.psum(contract_rows(vectors, block_t), ('sub', 'row'))  80.5 us
    psum x1, blocking collectives, per_device(): gram = lax.psum(contract_rows(twice, twice), ('sub', 'row')) / total_rows  74.4 us
    psum x1, blocking collectives, second_sum(): return lax.psum(inner, ('sub', 'row'))  72.9 us
    psum x1, waiting for transfers between devices, per_device(): summed = lax.psum(partial_value, 'row')  50.1 us
    ppermute x4, starting transfers between devices, from_behind(): lax.ppermute(value, axis, [(source, source + steps) for source in range(l...  15 us
    all_gather x1, blocking collectives, per_device(): whole = lax.all_gather(own_rows, 'row', axis=1, tiled=True)  14.5 us
    dot_general x4, matrix products, contract_rows(): lax.dot_general(left_mat, right_mat, (((1,), (1,)), ((), ())), precision=...  12.6 us
    ppermute x4, waiting for transfers between devices, from_behind(): lax.ppermute(value, axis, [(source, source + steps) for source in range(l...  8.3 us
  transfers between devices with their start and end apart: 5, of which 3 were waited for; matrix products, arithmetic and copies ran while one was open for 1% of the time, Pallas kernels for 0%

commit v1 on v0

--- a/solution.py
+++ b/solution.py
@@ -65,7 +65,7 @@
     inner_two = contract_rows(vectors, once)
     second = second_sum(inner_two)
     twice = once - contract_first(second, vectors)
-    gram = lax.psum(contract_rows(twice, twice), ("sub", "row")) / total_rows
+    gram = jnp.sum(lax.all_gather(contract_rows(twice, twice), ("sub", "row")), axis=0) / total_rows
     lower_tri = jnp.linalg.cholesky(gram)
     solved = jax.scipy.linalg.solve_triangular(lower_tri, twice, lower=True)
     return (first + second, lower_tri.T, solved[:, None, :])

time: 368 us -> 409 us (1.11)
  waiting for transfers between devices: 58.4 us -> 171 us
  blocking collectives: 242 us -> 168 us
    all_gather x0 -> x1, waiting for transfers between devices: none -> 113 us  [per_device(): lax.all_gather(contract_rows(twice, twice), ('sub', 'row'))]
    psum x1 -> x0, blocking collectives: 74.4 us -> none  [per_device(): gram = lax.psum(contract_rows(twice, twice), ('sub', 'row')) / total_rows]
  transfers between devices with their start and end apart: 5 -> 6, of which waited for: 3 -> 4; matrix products, arithmetic and copies ran while one was open for 1% -> 1% of each run, Pallas kernels for 0% -> 0%
where the time goes in v1:
time: 409 us; the launch traced here: 408 us
  waiting for transfers between devices  171 us (42%)
  blocking collectives  168 us (41%)
  matrix products  23.2 us (6%)
  starting transfers between devices  15.1 us (4%)
  between operations  14.3 us (3%)
  other arithmetic  10.1 us (2%)
  local copies, waits for them, and re-layouts  6.64 us (2%)
    all_gather x1, waiting for transfers between devices, per_device(): lax.all_gather(contract_rows(twice, twice), ('sub', 'row'))  113 us
    psum x1, blocking collectives, per_device(): first = lax.psum(contract_rows(vectors, block_t), ('sub', 'row'))  80.5 us
    psum x1, blocking collectives, second_sum(): return lax.psum(inner, ('sub', 'row'))  72.9 us
    psum x1, waiting for transfers between devices, per_device(): summed = lax.psum(partial_value, 'row')  50.1 us
    ppermute x4, starting transfers between devices, from_behind(): lax.ppermute(value, axis, [(source, source + steps) for source in range(l...  15 us
    all_gather x1, blocking collectives, per_device(): whole = lax.all_gather(own_rows, 'row', axis=1, tiled=True)  14.5 us
    dot_general x4, matrix products, contract_rows(): lax.dot_general(left_mat, right_mat, (((1,), (1,)), ((), ())), precision=...  13.2 us
    ppermute x4, waiting for transfers between devices, from_behind(): lax.ppermute(value, axis, [(source, source + steps) for source in range(l...  8.29 us
  transfers between devices with their start and end apart: 6, of which 4 were waited for; matrix products, arithmetic and copies ran while one was open for 1% of the time, Pallas kernels for 0%

profile of v1, /device:TPU:1, one launch (start us, length us, event | category | flops | bytes accessed | tf_op | source)
XLA Modules:
  0.0 408.1 jit_solution(868761952216870104)
XLA Ops:
  7.2 0.0 all-reduce.2.cloned.1.call-start
  7.2 0.8 fusion.30
  8.0 1.0 copy.11
  9.0 14.5 %all-gather = f32[32,1,2048]{0,2,1:T(8,128)S(1)} all-gather(f32[32,1,512]{0,2,1:T(8,128)S(1)} %copy.11), channel_id=2, replica_groups=mesh['sub'=64,'row'=4] {'row'}, dimensions={2}, use_global_device_ids=true | all-gather | bytes 327680 | tf_op jit(solution)/shard_map/all_gather | solution.py:33
  23.5 1.0 gather_fusion
  24.5 0.1 select_bitcast_fusion.1
  24.6 5.2 %collective-permute-start = (f32[32,512]{0,1:T(8,128)S(1)}, f32[32,512]{0,1:T(8,128)S(1)}, u32[]{:S(2)}, u32[]{:S(2)}) collective-permute-start(f32[32,512]{0,1:T(8,128)S(1)} %select_bitcast_fusion.1), channel_id=1, source_target_pairs={{0,4},{4,8},{8,12},{12,16},{16,20},{20,24},{24,28},{28,32},{32,36}... | collective-permute-start | bytes 196616 | tf_op jit(solution)/shard_map/ppermute | solution.py:12
  29.9 1.0 gather_fusion.1
  30.9 0.1 select_bitcast_fusion
  31.0 1.9 collective-permute-start.1
  33.0 0.3 copy.12
  33.3 0.0 collective-permute-done
  33.3 0.1 copy.13
  33.4 5.3 %collective-permute-done.1 = f32[32,512]{0,1:T(8,128)S(1)} collective-permute-done((f32[32,512]{0,1:T(8,128)S(1)}, f32[32,512]{0,1:T(8,128)S(1)}, u32[]{:S(2)}, u32[]{:S(2)}) %collective-permute-start.1) | collective-permute-done | bytes 65568 | tf_op jit(solution)/shard_map/ppermute | solution.py:12
  38.7 0.1 copy.14
  38.8 0.0 copy-start
  38.8 0.0 copy-start.1
  38.8 11.7 %fusion.1 = f32[32,768]{1,0:T(8,128)S(1)} fusion(f32[1,768,3072]{2,1,0:T(8,128)} %param.7, s32[768]{0:T(1024)S(1)} %iota_add_fusion, f32[32,512]{1,0:T(8,128)S(1)} %copy.14, f32[32,512]{1,0:T(8,128)S(1)} %copy.13, f32[32,2048]{1,0:T(8,128)S(1)} %copy.12), kind=kOutput, calls=%fused_computation.5 | convolution fusion | flops 913244160 | bytes 9931776 | tf_op jit(solution)/shard_map/dot_general | solution.py:16
  50.6 0.0 copy-done
  50.6 7.4 %fusion = f32[32,3072]{1,0:T(8,128)} fusion(f32[32,768]{1,0:T(8,128)S(1)} %fusion.1, f32[1,768,3072]{2,1,0:T(8,128)S(1)} %copy-done, s32[768]{0:T(1024)S(1)} %iota_add_fusion), kind=kOutput, calls=%fused_computation.4 | convolution fusion | flops 913047552 | bytes 9931776 | tf_op jit(solution)/shard_map/dot_general | solution.py:48
  58.0 0.0 all-reduce.2.cloned.1.call-update
  58.0 0.0 all-gather.4.cloned.1.call-start
  58.1 50.1 %all-reduce.2.cloned.1.call-done = f32[32,3072]{1,0:T(8,128)} async-done(((f32[32,3072]{1,0:T(8,128)}), f32[32,3072]{1,0:T(8,128)}) %all-reduce.2.cloned.1.call-update) | async-done | bytes 393232 | tf_op jit(solution)/shard_map/psum | solution.py:49
  108.2 0.9 fusion.29
  109.1 5.8 %collective-permute-start.3 = (f32[32,512]{1,0:T(8,128)S(1)}, f32[32,512]{1,0:T(8,128)S(1)}, u32[]{:S(2)}, u32[]{:S(2)}) collective-permute-start(f32[32,512]{1,0:T(8,128)S(1)} %get-tuple-element.11), channel_id=1, source_target_pairs={{0,4},{4,8},{8,12},{12,16},{16,20},{20,24},{24,28},{28,32},{32,36}... | collective-permute-start | bytes 196616 | tf_op jit(solution)/shard_map/ppermute | solution.py:12
  114.9 2.1 collective-permute-start.2
  117.0 0.0 collective-permute-done.3
  117.0 0.5 fusion.5
  117.5 3.0 collective-permute-done.2
  120.5 1.4 fusion.4
  121.9 0.0 copy-done.1
  121.9 0.3 convolution_bitcast_fusion.2
  122.2 80.5 %psum.22 = f32[96,32]{0,1:T(8,128)S(1)} all-reduce(f32[96,32]{0,1:T(8,128)S(1)} %convolution_bitcast_fusion.2), channel_id=1, replica_groups=mesh['sub'=64,'row'=4] {'sub','row'}, use_global_device_ids=true, to_apply=%region_1.3 | all-reduce | flops 3072 | bytes 24576 | tf_op jit(solution)/shard_map/psum | solution.py:63
  202.7 0.2 convolution_subtract_fusion.1
  202.9 0.3 convolution_bitcast_fusion.1
  203.3 72.9 %psum.23 = f32[96,32]{0,1:T(8,128)S(1)} all-reduce(f32[96,32]{0,1:T(8,128)S(1)} %convolution_bitcast_fusion.1), channel_id=1, replica_groups=mesh['sub'=64,'row'=4] {'sub','row'}, use_global_device_ids=true, to_apply=%region_2.4 | all-reduce | flops 3072 | bytes 24576 | tf_op jit(solution)/shard_map/psum | solution.py:24
  276.1 0.2 convolution_subtract_fusion
  276.3 0.8 fusion.31
  277.1 0.0 all-gather.4.cloned.1.call-update
  277.2 0.6 add.66
  277.8 112.5 %all-gather.4.cloned.1.call-done = f32[8192,32]{1,0:T(8,128)} async-done(((f32[32,32]{1,0:T(8,128)}), f32[8192,32]{1,0:T(8,128)}) %all-gather.4.cloned.1.call-update) | async-done | bytes 1048592 | tf_op jit(solution)/shard_map/all_gather | solution.py:68
  390.3 2.5 reduce_sum.11
  392.8 0.1 copy.15
  392.9 2.9 cholesky.18
  395.9 0.6 compare_reduce_fusion
  396.5 0.7 select_bitcast_fusion.2
  397.2 2.4 custom-call.7
  399.6 0.3 convolution_bitcast_fusion
  399.9 0.7 copy.17
  400.6 0.7 copy.16
  (10 shorter events, 0.1 us)
Async XLA Ops:
  7.2 101.0 %all-reduce.2.cloned.1.call-start = ((), (), s32[]{:S(2)}) async-start(), calls=%async_computation | async-start | bytes 786432 | tf_op jit(solution)/shard_map/psum | solution.py:49
  24.6 8.6 %collective-permute-start = (f32[32,512]{0,1:T(8,128)S(1)}, f32[32,512]{0,1:T(8,128)S(1)}, u32[]{:S(2)}, u32[]{:S(2)}) collective-permute-start(f32[32,512]{0,1:T(8,128)S(1)} %select_bitcast_fusion.1), channel_id=1, source_target_pairs={{0,4},{4,8},{8,12},{12,16},{16,20},{20,24},{24,28},{28,32},{32,36}... | collective-permute-start | bytes 196616 | tf_op jit(solution)/shard_map/ppermute | solution.py:12
  31.0 7.7 %collective-permute-start.1 = (f32[32,512]{0,1:T(8,128)S(1)}, f32[32,512]{0,1:T(8,128)S(1)}, u32[]{:S(2)}, u32[]{:S(2)}) collective-permute-start(f32[32,512]{0,1:T(8,128)S(1)} %select_bitcast_fusion), channel_id=1, source_target_pairs={{4,0},{8,4},{12,8},{16,12},{20,16},{24,20},{28,24},{32,28},{36,32}... | collective-permute-start | bytes 196616 | tf_op jit(solution)/shard_map/ppermute | solution.py:12
  38.8 11.8 %copy-start = (f32[1,768,3072]{2,1,0:T(8,128)S(1)}, f32[1,768,3072]{2,1,0:T(8,128)}, u32[]{:S(2)}) copy-start(f32[1,768,3072]{2,1,0:T(8,128)} %param.7) | copy-start | bytes 28311556
  38.8 83.0 %copy-start.1 = (f32[96,1,512]{2,1,0:T(1,128)S(1)}, f32[96,1,512]{2,1,0:T(1,128)}, u32[]{:S(2)}) copy-start(f32[96,1,512]{2,1,0:T(1,128)} %param.8) | copy-start | bytes 589828
  58.0 332.3 %all-gather.4.cloned.1.call-start = ((), (), s32[]{:S(2)}) async-start(), calls=%async_computation.1 | async-start | bytes 4210688 | tf_op jit(solution)/shard_map/all_gather | solution.py:68
  109.1 8.0 %collective-permute-start.3 = (f32[32,512]{1,0:T(8,128)S(1)}, f32[32,512]{1,0:T(8,128)S(1)}, u32[]{:S(2)}, u32[]{:S(2)}) collective-permute-start(f32[32,512]{1,0:T(8,128)S(1)} %get-tuple-element.11), channel_id=1, source_target_pairs={{0,4},{4,8},{8,12},{12,16},{16,20},{20,24},{24,28},{28,32},{32,36}... | collective-permute-start | bytes 196616 | tf_op jit(solution)/shard_map/ppermute | solution.py:12
  114.9 5.6 %collective-permute-start.2 = (f32[32,512]{1,0:T(8,128)S(1)}, f32[32,512]{1,0:T(8,128)S(1)}, u32[]{:S(2)}, u32[]{:S(2)}) collective-permute-start(f32[32,512]{1,0:T(8,128)S(1)} %get-tuple-element.10), channel_id=1, source_target_pairs={{4,0},{8,4},{12,8},{16,12},{20,16},{24,20},{28,24},{32,28},{36,32}... | collective-permute-start | bytes 196616 | tf_op jit(solution)/shard_map/ppermute | solution.py:12
Sparse Core Ops, SparseCore 0:
  58.2 49.9 all-reduce.1
  277.3 112.9 all-gather.3
